TPU v7x, 32 devices: a whole 2x2x4 slice. The times are simulated.
32 devices in a mesh: ctx: 16 (over z, y, x), head: 2 (over core).
Axes of the slice: x: 2, y: 2, z: 4, core: 2. Of those that a mesh axis runs over, the one named last changes fastest.
Arguments:
- queries: bfloat16 [4096, 4096], P('ctx', 'head')
- keys: bfloat16 [4096, 1024], P('ctx', 'head')
- values: bfloat16 [4096, 1024], P('ctx', 'head'), may hold values from -6 to 6
- positions: int32 [4096], P('ctx'), may hold values from 0 to 6143, as said below
- retrieval: int32 [4], replicated, may hold values from 0 to 7, as said below
- yarn_scale: int32 [1], replicated, may hold values from 2 to 8
- out_weight: bfloat16 [4096, 4096], P('head', 'ctx'), may hold values from -0.125 to 0.125
Outputs:
- layer_out: bfloat16 [4096, 4096], P('ctx', 'head')
Inputs may be any that keep to these rules, and one draw needn't show every extreme that they name: positions start at 0 and rise by 1 or 2 from one token to the next, by 2 at exactly 2048 of the steps. `retrieval`: 4 different KV-head indices.
All inputs are finite; a program needn't handle non-finite values.
Results may differ from a plain program's by a relative error of at most 0.014.
The roundings to bfloat16 on the way count: a program that leaves them out, or rounds other values in their place, can miss the bound.
Values may be sent and summed in bfloat16 or wider, within the bound.
No kernel may reach another device: no remote copies, remote signals or barrier semaphores. Data moves between devices by JAX's collectives and lax.ppermute only.
A program may use at most 128 MiB of HBM per device.

v0:
```python
from functools import partial
import math
import jax
import jax.numpy as jnp
from jax import lax
from jax.sharding import Mesh, PartitionSpec as P

HEAD_SIZE = 128
SINK = 64
WINDOW = 256
ORIG_CTX = 8192
QUERY_PER_KEY = 4
rope_base = 500000.0
neg_big = -1e30


def yarn_tables(positions, yarn_scale):
    half_size = HEAD_SIZE // 2
    factor = yarn_scale[0].astype(jnp.float32)
    freq_index = jnp.arange(half_size, dtype=jnp.float32)
    base_freq = jnp.power(jnp.float32(rope_base), -2.0 * freq_index / HEAD_SIZE)
    wave_ratio = ORIG_CTX * base_freq / (2.0 * math.pi)
    ramp_weight = jnp.clip((wave_ratio - 1.0) / 31.0, 0.0, 1.0)
    yarn_freq = base_freq * ramp_weight + base_freq / factor * (1.0 - ramp_weight)
    angles = positions.astype(jnp.float32)[:, None] * yarn_freq[None, :]
    mscale = 0.1 * jnp.log(factor) + 1.0
    return (jnp.cos(angles) * mscale, jnp.sin(angles) * mscale)


def apply_rotary(x, cosine_lookup, sine_lookup, head_count):
    row_count = x.shape[0]
    shaped = x.astype(jnp.float32).reshape(row_count, head_count, HEAD_SIZE)
    lower_half = shaped[..., : HEAD_SIZE // 2]
    upper_half = shaped[..., HEAD_SIZE // 2 :]
    cosine = cosine_lookup[:, None, :]
    sine_part = sine_lookup[:, None, :]
    rotated = jnp.concatenate(
        [
            lower_half * cosine - upper_half * sine_part,
            upper_half * cosine + lower_half * sine_part,
        ],
        axis=-1,
    )
    return rotated.reshape(row_count, head_count * HEAD_SIZE).astype(jnp.bfloat16)


def update(query_rows, key_block, value_block, visible, partial_state):
    row_max, totals, accum = partial_state
    scores = jnp.einsum(
        "rhgd,khd->hgrk", query_rows, key_block, preferred_element_type=jnp.float32
    ) * (1.0 / math.sqrt(HEAD_SIZE))
    mask_full = visible[:, None]
    scores = jnp.where(mask_full, scores, neg_big)
    new_max = jnp.maximum(row_max, jnp.max(scores, axis=-1))
    weights = jnp.where(mask_full, jnp.exp(scores - new_max[..., None]), 0.0)
    rescale = jnp.exp(row_max - new_max)
    totals = totals * rescale + jnp.sum(weights, axis=-1)
    accum = accum * rescale[..., None] + jnp.einsum(
        "hgrk,khd->hgrd",
        weights.astype(jnp.bfloat16),
        value_block,
        preferred_element_type=jnp.float32,
    )
    return (new_max, totals, accum)


def attend(query_sets, rotated_key, values, flags, kv_local):
    shaped_sets = []
    initial = []
    for query_rows, query_index in query_sets:
        row_count = query_rows.shape[0]
        shaped_sets.append(
            (query_rows.reshape(row_count, kv_local, QUERY_PER_KEY, HEAD_SIZE), query_index)
        )
        initial.append(
            (
                jnp.full((kv_local, QUERY_PER_KEY, row_count), neg_big, jnp.float32),
                jnp.zeros((kv_local, QUERY_PER_KEY, row_count), jnp.float32),
                jnp.zeros((kv_local, QUERY_PER_KEY, row_count, HEAD_SIZE), jnp.float32),
            )
        )
    initial = tuple(initial)
    kv_width = rotated_key.shape[1]
    kv_shard = lax.all_gather(
        jnp.concatenate([rotated_key, values], axis=1), CTX, axis=0, tiled=True
    )
    key_shard = kv_shard[:, :kv_width]
    value_shard = kv_shard[:, kv_width:]
    shard_rows = key_shard.shape[0]
    sub_rows = math.gcd(shard_rows, 512)
    turn_count = shard_rows // sub_rows

    def one_turn(j, inner_states):
        key_block = lax.dynamic_slice_in_dim(key_shard, j * sub_rows, sub_rows, 0).reshape(
            sub_rows, kv_local, HEAD_SIZE
        )
        value_block = lax.dynamic_slice_in_dim(value_shard, j * sub_rows, sub_rows, 0).reshape(
            sub_rows, kv_local, HEAD_SIZE
        )
        key_index = j * sub_rows + jnp.arange(sub_rows, dtype=jnp.int32)
        updated = []
        for (query_rows, query_index), partial_state in zip(shaped_sets, inner_states):
            causal = key_index[None, :] <= query_index[:, None]
            nearby = (key_index[None, :] < SINK) | (
                key_index[None, :] > query_index[:, None] - WINDOW
            )
            visible = causal[None] & (flags[:, None, None] | nearby[None])
            updated.append(
                lax.cond(
                    jnp.any(visible),
                    partial(update, query_rows, key_block, value_block, visible),
                    lambda keep_state: keep_state,
                    partial_state,
                )
            )
        return tuple(updated)

    final = lax.fori_loop(0, turn_count, one_turn, initial)
    results = []
    for (query_rows, query_index), (row_max, totals, accum) in zip(shaped_sets, final):
        output = accum / totals[..., None]
        results.append(
            output.transpose(2, 0, 1, 3)
            .reshape(query_rows.shape[0], kv_local * QUERY_PER_KEY * HEAD_SIZE)
            .astype(jnp.bfloat16)
        )
    return results


CTX = ("cz", "cb")


def head_exchange(x, head_count):
    if head_count == 2:
        other = lax.ppermute(x, "head", [(0, 1), (1, 0)])
        first = lax.axis_index("head") == 0
        return jnp.stack([jnp.where(first, x, other), jnp.where(first, other, x)])
    return lax.all_gather(x, "head", axis=0, tiled=False)


def duo_attend(rotated_query, rotated_key, values, retrieval, kv_local, head_count, ctx_index):
    rows = rotated_query.shape[0]
    ctx_count = lax.psum(1, CTX)
    kv_total = kv_local * head_count
    ret_count = retrieval.shape[0]
    ret_per = ret_count // head_count
    run_per = (kv_total - ret_count) // head_count
    me = lax.axis_index("head")
    is_ret = jnp.any(jnp.arange(kv_total, dtype=jnp.int32)[:, None] == retrieval[None, :], axis=1)
    order = jnp.argsort(is_ret.astype(jnp.int32), stable=True)
    run_ids = lax.dynamic_slice_in_dim(order, me * run_per, run_per)
    ret_ids = lax.dynamic_slice_in_dim(order, kv_total - ret_count + me * ret_per, ret_per)
    q_all = head_exchange(
        rotated_query.reshape(rows, kv_local, QUERY_PER_KEY, HEAD_SIZE), head_count
    )
    q_all = q_all.transpose(1, 0, 2, 3, 4).reshape(rows, kv_total, QUERY_PER_KEY, HEAD_SIZE)
    kv_own = jnp.stack(
        [rotated_key.reshape(rows, kv_local, HEAD_SIZE), values.reshape(rows, kv_local, HEAD_SIZE)],
        axis=2,
    )
    kv_all = head_exchange(kv_own, head_count)
    kv_all = kv_all.transpose(1, 0, 2, 3, 4).reshape(rows, kv_total, 2, HEAD_SIZE)
    own_index = ctx_index * rows + jnp.arange(rows, dtype=jnp.int32)
    inv_root = 1.0 / math.sqrt(HEAD_SIZE)
    run_kv = jnp.take(kv_all, run_ids, axis=1)
    prev_kv = lax.ppermute(run_kv, CTX, [(i, i + 1) for i in range(ctx_count - 1)])
    sink_kv = lax.psum(jnp.where(ctx_index == 0, run_kv[:SINK], jnp.zeros_like(run_kv[:SINK])), CTX)
    near_kv = jnp.concatenate([sink_kv, prev_kv, run_kv], axis=0)
    sink_index = jnp.arange(SINK, dtype=jnp.int32)
    window_index = (ctx_index - 1) * rows + jnp.arange(2 * rows, dtype=jnp.int32)
    causal_sink = sink_index[None, :] <= own_index[:, None]
    in_window = (
        (window_index[None, :] <= own_index[:, None])
        & (window_index[None, :] > own_index[:, None] - WINDOW)
        & (window_index[None, :] >= SINK)
    )
    near_visible = jnp.concatenate([causal_sink, in_window], axis=1)[None]
    q_run = jnp.take(q_all, run_ids, axis=1)
    start = (
        jnp.full((run_per, QUERY_PER_KEY, rows), neg_big, jnp.float32),
        jnp.zeros((run_per, QUERY_PER_KEY, rows), jnp.float32),
        jnp.zeros((run_per, QUERY_PER_KEY, rows, HEAD_SIZE), jnp.float32),
    )
    _, run_totals, run_accum = update(
        q_run, near_kv[:, :, 0], near_kv[:, :, 1], near_visible, start
    )
    run_out = run_accum / run_totals[..., None]
    ret_kv = jnp.take(kv_all, ret_ids, axis=1)
    ret_shard = lax.all_gather(
        ret_kv.reshape(rows, ret_per * 2 * HEAD_SIZE), CTX, axis=0, tiled=True
    )
    ret_shard = ret_shard.reshape(ctx_count * rows, ret_per, 2, HEAD_SIZE)
    q_ret = jnp.take(q_all, ret_ids, axis=1)
    sub_rows = math.gcd(ctx_count * rows, 512)
    turn_count = (ctx_index * rows + rows + sub_rows - 1) // sub_rows

    def one_turn(j, state):
        block = lax.dynamic_slice_in_dim(ret_shard, j * sub_rows, sub_rows, 0)
        key_index = j * sub_rows + jnp.arange(sub_rows, dtype=jnp.int32)
        visible = (key_index[None, :] <= own_index[:, None])[None]
        return update(q_ret, block[:, :, 0], block[:, :, 1], visible, state)

    start = (
        jnp.full((ret_per, QUERY_PER_KEY, rows), neg_big, jnp.float32),
        jnp.zeros((ret_per, QUERY_PER_KEY, rows), jnp.float32),
        jnp.zeros((ret_per, QUERY_PER_KEY, rows, HEAD_SIZE), jnp.float32),
    )
    _, ret_totals, ret_accum = lax.fori_loop(0, turn_count, one_turn, start)
    ret_out = ret_accum / ret_totals[..., None]
    done = jnp.concatenate([ret_out, run_out], axis=0).astype(jnp.bfloat16)
    slots = head_exchange(done, head_count).reshape(kv_total, QUERY_PER_KEY, rows, HEAD_SIZE)
    placed = jnp.concatenate(
        [
            jnp.concatenate(
                [
                    order[
                        kv_total
                        - ret_count
                        + h * ret_per : kv_total
                        - ret_count
                        + (h + 1) * ret_per
                    ],
                    order[h * run_per : (h + 1) * run_per],
                ]
            )
            for h in range(head_count)
        ]
    )
    slot_of = jnp.argsort(placed)
    home = jnp.take(slots, lax.dynamic_slice_in_dim(slot_of, me * kv_local, kv_local), axis=0)
    return home.transpose(2, 0, 1, 3).reshape(rows, kv_local * QUERY_PER_KEY * HEAD_SIZE)


def project(attended, w_local, head_count):
    rows = attended.shape[0]
    col_width = w_local.shape[1]
    plane = lax.psum(1, "cb")
    line = lax.psum(1, "cz")
    a_plane = lax.all_gather(attended, "cb", axis=0, tiled=True)
    w_line = lax.all_gather(w_local, "cz", axis=1, tiled=True)
    part = jnp.dot(a_plane, w_line, preferred_element_type=jnp.float32)
    reduced = lax.psum_scatter(part, "head", scatter_dimension=1, tiled=True).astype(jnp.bfloat16)
    per_head = line // head_count
    pieces = reduced.reshape(plane, rows, per_head * col_width)
    got = lax.all_to_all(pieces, "cb", 0, 0, tiled=False)
    return (
        got.reshape(plane, rows, per_head, col_width)
        .transpose(1, 2, 0, 3)
        .reshape(rows, per_head * plane * col_width)
    )


def shards(queries, keys, values, positions, retrieval, yarn_scale, out_weight):
    rows_dev = queries.shape[0]
    kv_local = keys.shape[1] // HEAD_SIZE
    cosine_lookup, sine_lookup = yarn_tables(positions, yarn_scale)
    rotated_query = apply_rotary(queries, cosine_lookup, sine_lookup, kv_local * QUERY_PER_KEY)
    rotated_key = apply_rotary(keys, cosine_lookup, sine_lookup, kv_local)
    ctx_index = lax.axis_index("cz") * lax.psum(1, "cb") + lax.axis_index("cb")
    head_ids = lax.axis_index("head") * kv_local + jnp.arange(kv_local, dtype=jnp.int32)
    flags = jnp.any(head_ids[:, None] == retrieval[None, :], axis=1)
    own_index = ctx_index * rows_dev + jnp.arange(rows_dev, dtype=jnp.int32)
    head_count = lax.psum(1, "head")
    kv_total = kv_local * head_count
    ret_count = retrieval.shape[0]
    if (
        ret_count % head_count == 0
        and (kv_total - ret_count) % head_count == 0
        and (ret_count < kv_total)
        and (rows_dev >= max(SINK, WINDOW))
    ):
        attended = duo_attend(
            rotated_query, rotated_key, values, retrieval, kv_local, head_count, ctx_index
        )
    else:
        attended = attend(((rotated_query, own_index),), rotated_key, values, flags, kv_local)[0]
    return project(attended, out_weight, head_count)


def grid_of(ctx_count, head_count):
    best = None
    for plane in range(1, ctx_count + 1):
        line = ctx_count // plane
        if ctx_count % plane == 0 and line % head_count == 0 and (plane <= line):
            best = (line, plane)
    return best


def solution(mesh):
    ctx_count = mesh.shape["ctx"]
    head_count = mesh.shape["head"]
    line, plane = grid_of(ctx_count, head_count)
    grid = Mesh(mesh.devices.reshape(line, plane, head_count), ("cz", "cb", "head"))
    return jax.shard_map(
        shards,
        mesh=grid,
        in_specs=(P(CTX, "head"), P(CTX, "head"), P(CTX, "head"), P(CTX), P(), P(), P("head", CTX)),
        out_specs=P(CTX, "head"),
        check_vma=False,
    )
```

profile of v0, /device:TPU:0, one launch (start us, length us, event | category | flops | bytes accessed | tf_op | source)
XLA Modules:
  0.0 394.5 jit_solution(9107826275673010215)
XLA Ops:
  7.2 0.7 convert_element_type.38
  7.9 1.1 copy.33
  9.0 1.1 copy.32
  10.2 0.3 fusion.36
  10.6 0.6 collective-permute-start
  11.2 0.7 fusion.38
  11.9 1.0 sort.34
  13.0 0.2 select_bitcast_fusion.7
  13.3 0.7 copy.34
  14.0 0.6 gather_fusion.3
  14.7 0.6 slice_select_fusion
  15.4 0.6 gather_fusion.1
  16.1 0.9 copy.35
  17.3 0.2 convert_bitcast_fusion
  17.5 0.4 copy.54
  17.9 0.7 fusion.45
  18.6 1.4 subtract_convert_fusion
  20.0 0.6 pad_maximum_fusion.2
  20.8 0.2 and_and_fusion
  21.0 5.5 %collective-permute-start.2 = (bf16[256,2,2,128]{3,0,1,2:T(8,128)(2,1)S(1)}, bf16[256,2,2,128]{3,0,1,2:T(8,128)(2,1)}, u32[]{:S(2)}, u32[]{:S(2)}) collective-permute-start(bf16[256,2,2,128]{3,0,1,2:T(8,128)(2,1)S(1)} %fusion.32), channel_id=1, source_target_pairs={{0,2},{2,4},{4,6},{6,8},{8,10},{10,12},{12,14},{14,16},{16,18},{18... | collective-permute-start | bytes 786440 | tf_op jit(solution)/shard_map/ppermute | solution.py:166
  26.6 94.8 %all-reduce.2.cloned.1.call-done = bf16[64,2,2,128]{3,0,1,2:T(8,128)(2,1)} async-done(((bf16[64,2,2,128]{3,0,1,2:T(8,128)(2,1)}), bf16[64,2,2,128]{3,0,1,2:T(8,128)(2,1)}) %all-reduce.2.cloned.1.call-update) | async-done | bytes 65552 | tf_op jit(solution)/shard_map/psum | solution.py:167
  121.4 1.0 pad_maximum_fusion.4
  122.6 0.2 pad_maximum_fusion
  122.8 1.4 gather_fusion.4
  124.2 0.6 gather_fusion.2
  124.8 2.0 fusion.17
  126.8 1.2 fusion.18
  128.1 2.0 divide_convert_fusion
  130.2 79.8 %all-gather.4.cloned.1.call-done = bf16[4096,512]{0,1:T(8,128)(2,1)} async-done(((bf16[256,512]{0,1:T(8,128)(2,1)}), bf16[4096,512]{0,1:T(8,128)(2,1)}) %all-gather.4.cloned.1.call-update) | async-done | bytes 4194320 | tf_op jit(solution)/shard_map/all_gather | solution.py:189
  210.0 9.7 %while.15 = (s32[]{:T(128)}, f32[2,4,256]{2,1,0:T(4,128)S(1)}, f32[2,4,256]{2,1,0:T(4,128)S(1)}, f32[2,4,256,128]{3,2,1,0:T(8,128)S(1)}, s32[]{:T(128)}, /*index...) while((s32[]{:T(128)}, f32[2,4,256]{2,1,0:T(4,128)S(1)}, ...), condition=%wide.region_6.9_spmd.clone, body=%wide.region_3.8_spmd.clone.sunk | while | flops 551162624 | bytes 33167600 | solution.py:208
  210.4 1.8 fusion.58
  212.3 1.9 copy-done
  214.3 1.0 fusion.59
  215.3 4.4 %fusion.60 = f32[2,4,256,128]{3,2,1,0:T(8,128)S(1)} fusion(f32[2,512,256,4]{2,1,3,0:T(8,128)} %copy-done, f32[2,4,256]{2,1,0:T(4,128)S(1)} %max.13, pred[256,512]{0,1:T(8,128)(4,1)S(1)} %broadcast_compare_fusion.3, f32[2,4,256,128]{3,2,1,0:T(8,128)S(1)} %get-tuple-element.231, f32[2,4,256]{2,1,0:T(4,128)S(1)} %bitcast.163, ...), kind=kOutput, calls=%fused_computation.13.clone.1 | convolution fusion | flops 274202624 | bytes 6701064 | tf_op jit(solution)/shard_map/while/body/hgrk,khd->hgrd/dot_general | solution.py:58
  219.7 0.3 divide_convert_fusion.1
  220.4 1.0 sort.35
  221.4 1.4 collective-permute-done.3
  223.2 0.7 gather_fusion
  224.2 1.3 copy.42
  225.5 64.7 %all-gather.8.cloned.1.call-done = bf16[2048,1024]{1,0:T(8,128)(2,1)} async-done(((bf16[2048,256]{1,0:T(8,128)(2,1)}), bf16[2048,1024]{1,0:T(8,128)(2,1)}) %all-gather.8.cloned.1.call-update) | async-done | bytes 4194320 | tf_op jit(solution)/shard_map/all_gather | solution.py:240
  290.3 52.3 %all-gather.6.cloned.1.call-done = bf16[1024,2048]{0,1:T(8,128)(2,1)} async-done(((bf16[256,2048]{0,1:T(8,128)(2,1)}), bf16[1024,2048]{0,1:T(8,128)(2,1)}) %all-gather.6.cloned.1.call-update) | async-done | bytes 4194320 | tf_op jit(solution)/shard_map/all_gather | solution.py:239
  342.6 10.0 %fusion.47 = f32[1024,1024]{1,0:T(8,128)} fusion(bf16[1024,2048]{0,1:T(8,128)(2,1)} %all-gather.6.cloned.1.call-done, bf16[2048,1024]{1,0:T(8,128)(2,1)} %all-gather.8.cloned.1.call-done), kind=kOutput, calls=%fused_computation.105 | convolution fusion | flops 4294967296 | bytes 12582912 | tf_op jit(solution)/shard_map/dot_general | solution.py:241
  352.7 12.0 %reduce-scatter.2.cloned.1.call-done = f32[1024,512]{1,0:T(8,128)} async-done(((f32[1024,1024]{1,0:T(8,128)}), f32[1024,512]{1,0:T(8,128)}) %reduce-scatter.2.cloned.1.call-update) | async-done | bytes 2097168 | tf_op jit(solution)/shard_map/reduce_scatter | solution.py:242
  364.7 1.7 convert_element_type.43
  366.4 18.3 %all_to_all.5 = bf16[4,256,512]{2,1,0:T(8,128)(2,1)S(1)} all-to-all(bf16[4,256,512]{2,1,0:T(8,128)(2,1)S(1)} %bitcast.148), channel_id=1, replica_groups=mesh['cz'=4,'cb'=4,'head'=2] {'cb'}, dimensions={0} | all-to-all | bytes 2097152 | tf_op jit(solution)/shard_map/all_to_all | solution.py:245
  384.7 0.3 reshape.220
  385.0 1.4 copy.63
  386.3 1.6 reshape.221
  (59 shorter events, 2.6 us)
Async XLA Ops:
  6.5 114.9 %all-reduce.2.cloned.1.call-start = ((), (), s32[]{:S(2)}) async-start(), calls=%async_computation.3 | async-start | bytes 131072 | tf_op jit(solution)/shard_map/psum | solution.py:167
  10.6 2.4 collective-permute-start
  13.2 4.1 %copy-start.1 = (bf16[256,2048]{1,0:T(8,128)(2,1)S(1)}, bf16[256,2048]{1,0:T(8,128)(2,1)}, u32[]{:S(2)}) copy-start(bf16[256,2048]{1,0:T(8,128)(2,1)} %param.13) | copy-start | bytes 3145732
  15.4 194.6 %all-gather.4.cloned.1.call-start = ((), (), s32[]{:S(2)}) async-start(), calls=%async_computation.2 | async-start | bytes 4456448 | tf_op jit(solution)/shard_map/all_gather | solution.py:189
  17.0 273.3 %all-gather.8.cloned.1.call-start = ((), (), s32[]{:S(2)}) async-start(), calls=%async_computation.5 | async-start | bytes 5242880 | tf_op jit(solution)/shard_map/all_gather | solution.py:240
  20.5 101.9 %collective-permute-start.1 = (bf16[256,4,4,128]{3,0,2,1:T(8,128)(2,1)S(1)}, bf16[256,4,4,128]{3,0,2,1:T(8,128)(2,1)S(1)}, u32[]{:S(2)}, u32[]{:S(2)}) collective-permute-start(bf16[256,4,4,128]{3,0,2,1:T(8,128)(2,1)S(1)} %bitcast.146), channel_id=1, source_target_pairs={{0,1},{1,0},{2,3},{3,2},{4,5},{5,4},{6,7},{7,6},{8,9},{9,8},{10,11... | collective-permute-start | bytes 3145736 | tf_op jit(solution)/shard_map/ppermute | solution.py:135
  20.7 321.9 %all-gather.6.cloned.1.call-start = ((), (), s32[]{:S(2)}) async-start(), calls=%async_computation.4 | async-start | bytes 5242880 | tf_op jit(solution)/shard_map/all_gather | solution.py:239
  21.0 100.4 %collective-permute-start.2 = (bf16[256,2,2,128]{3,0,1,2:T(8,128)(2,1)S(1)}, bf16[256,2,2,128]{3,0,1,2:T(8,128)(2,1)}, u32[]{:S(2)}, u32[]{:S(2)}) collective-permute-start(bf16[256,2,2,128]{3,0,1,2:T(8,128)(2,1)S(1)} %fusion.32), channel_id=1, source_target_pairs={{0,2},{2,4},{4,6},{6,8},{8,10},{10,12},{12,14},{14,16},{16,18},{18... | collective-permute-start | bytes 786440 | tf_op jit(solution)/shard_map/ppermute | solution.py:166
  212.3 2.0 copy-start
  220.2 2.7 collective-permute-start.3
  225.5 139.2 %reduce-scatter.2.cloned.1.call-start = ((), (), s32[]{:S(2)}) async-start(), calls=%async_computation.6 | async-start | bytes 6291456 | tf_op jit(solution)/shard_map/reduce_scatter | solution.py:242
Sparse Core Ops, SparseCore 0:
  15.5 105.8 all-reduce.1
  124.1 85.7 all-gather.3
  211.5 78.7 all-gather.7
  292.0 50.6 all-gather.5
  352.8 11.8 reduce-scatter.1
where the time goes:
time: 395 us; the launch traced here: 394 us
  waiting for transfers between devices  305 us (77%)
  matrix products  20.3 us (5%)
  blocking collectives  18.3 us (5%)
  local copies, waits for them, and re-layouts  15.6 us (4%)
  between operations  14.2 us (4%)
  other arithmetic  14.1 us (4%)
  starting transfers between devices  6.47 us (2%)
    psum x1, waiting for transfers between devices, duo_attend(): lax.psum(jnp.where(ctx_index == 0, run_kv[:SINK], jnp.zeros_like(run_kv[:...  94.8 us
    all_gather x1, waiting for transfers between devices, duo_attend(): lax.all_gather(ret_kv.reshape(rows, ret_per * 2 * HEAD_SIZE), CTX, axis=0...  79.8 us
    all_gather x1, waiting for transfers between devices, project(): w_line = lax.all_gather(w_local, 'cz', axis=1, tiled=True)  64.7 us
    all_gather x1, waiting for transfers between devices, project(): a_plane = lax.all_gather(attended, 'cb', axis=0, tiled=True)  52.3 us
    all_to_all x1, blocking collectives, project(): got = lax.all_to_all(pieces, 'cb', 0, 0, tiled=False)  18.3 us
    reduce_scatter x1, waiting for transfers between devices, project(): lax.psum_scatter(part, 'head', scatter_dimension=1, tiled=True)  12 us
    dot_general x1, matrix products, project(): part = jnp.dot(a_plane, w_line, preferred_element_type=jnp.float32)  10 us
  transfers between devices with their start and end apart: 9, of which 6 were waited for; matrix products, arithmetic and copies ran while one was open for 7% of the time, Pallas kernels for 0%

commit v1 on v0

--- a/solution.py
+++ b/solution.py
@@ -164,7 +164,12 @@
     inv_root = 1.0 / math.sqrt(HEAD_SIZE)
     run_kv = jnp.take(kv_all, run_ids, axis=1)
     prev_kv = lax.ppermute(run_kv, CTX, [(i, i + 1) for i in range(ctx_count - 1)])
-    sink_kv = lax.psum(jnp.where(ctx_index == 0, run_kv[:SINK], jnp.zeros_like(run_kv[:SINK])), CTX)
+    sink_kv = jnp.sum(
+        lax.all_gather(
+            jnp.where(ctx_index == 0, run_kv[:SINK], jnp.zeros_like(run_kv[:SINK])), CTX
+        ),
+        axis=0,
+    )
     near_kv = jnp.concatenate([sink_kv, prev_kv, run_kv], axis=0)
     sink_index = jnp.arange(SINK, dtype=jnp.int32)
     window_index = (ctx_index - 1) * rows + jnp.arange(2 * rows, dtype=jnp.int32)

time: 395 us -> 349 us (0.88)
  waiting for transfers between devices: 305 us -> 257 us
    psum x1 -> x0, waiting for transfers between devices: 94.8 us -> none  [duo_attend(): lax.psum(jnp.where(ctx_index == 0, run_kv[:SINK], jnp.zeros_like(run_kv[:...]
    all_gather x0 -> x1, waiting for transfers between devices: none -> 45.5 us  [duo_attend(): lax.all_gather(jnp.where(ctx_index == 0, run_kv[:SINK], jnp.zeros_like(ru...]
  transfers between devices with their start and end apart: 9 -> 9, of which waited for: 6 -> 6; matrix products, arithmetic and copies ran while one was open for 7% -> 8% of each run, Pallas kernels for 0% -> 0%
where the time goes in v1:
time: 349 us; the launch traced here: 348 us
  waiting for transfers between devices  257 us (74%)
  matrix products  19.9 us (6%)
  blocking collectives  18.3 us (5%)
  other arithmetic  16.2 us (5%)
  local copies, waits for them, and re-layouts  15.3 us (4%)
  between operations  14.3 us (4%)
  starting transfers between devices  6.45 us (2%)
    all_gather x1, waiting for transfers between devices, duo_attend(): lax.all_gather(ret_kv.reshape(rows, ret_per * 2 * HEAD_SIZE), CTX, axis=0...  81.1 us
    all_gather x1, waiting for transfers between devices, project(): w_line = lax.all_gather(w_local, 'cz', axis=1, tiled=True)  64.7 us
    all_gather x1, waiting for transfers between devices, project(): a_plane = lax.all_gather(attended, 'cb', axis=0, tiled=True)  52.3 us
    all_gather x1, waiting for transfers between devices, duo_attend(): lax.all_gather(jnp.where(ctx_index == 0, run_kv[:SINK], jnp.zeros_like(ru...  45.5 us
    all_to_all x1, blocking collectives, project(): got = lax.all_to_all(pieces, 'cb', 0, 0, tiled=False)  18.3 us
    reduce_scatter x1, waiting for transfers between devices, project(): lax.psum_scatter(part, 'head', scatter_dimension=1, tiled=True)  12 us
    dot_general x1, matrix products, project(): part = jnp.dot(a_plane, w_line, preferred_element_type=jnp.float32)  10 us
  transfers between devices with their start and end apart: 9, of which 6 were waited for; matrix products, arithmetic and copies ran while one was open for 8% of the time, Pallas kernels for 0%

profile of v1, /device:TPU:0, one launch (start us, length us, event | category | flops | bytes accessed | tf_op | source)
XLA Modules:
  0.0 348.0 jit_solution(9348527974595854793)
XLA Ops:
  7.2 0.7 convert_element_type.40
  7.9 1.1 copy.33
  9.0 1.1 copy.32
  10.2 0.3 fusion.36
  10.6 0.6 collective-permute-start
  11.2 0.7 fusion.38
  11.9 1.0 sort.34
  13.2 0.2 copy-done.2
  13.6 0.7 copy.34
  14.2 0.6 gather_fusion.3
  14.9 0.6 slice_select_fusion
  15.7 0.6 gather_fusion.1
  16.4 0.9 copy.35
  17.5 0.2 convert_bitcast_fusion
  17.8 0.4 copy.54
  18.2 0.7 fusion.45
  18.9 1.4 subtract_convert_fusion
  20.2 0.6 pad_maximum_fusion.2
  21.3 5.6 %collective-permute-start.2 = (bf16[256,2,2,128]{3,0,1,2:T(8,128)(2,1)S(1)}, bf16[256,2,2,128]{3,0,1,2:T(8,128)(2,1)}, u32[]{:S(2)}, u32[]{:S(2)}) collective-permute-start(bf16[256,2,2,128]{3,0,1,2:T(8,128)(2,1)S(1)} %fusion.32), channel_id=1, source_target_pairs={{0,2},{2,4},{4,6},{6,8},{8,10},{10,12},{12,14},{14,16},{16,18},{18... | collective-permute-start | bytes 786440 | tf_op jit(solution)/shard_map/ppermute | solution.py:166
  27.2 0.8 gather_fusion.4
  28.0 0.8 gather_fusion.2
  28.7 0.8 select_bitcast_fusion.5
  29.5 45.5 %all-gather.12.cloned.1.call-done = bf16[1024,2,2,128]{3,0,1,2:T(8,128)(2,1)} async-done(((bf16[64,2,2,128]{3,0,1,2:T(8,128)(2,1)}), bf16[1024,2,2,128]{3,0,1,2:T(8,128)(2,1)}) %all-gather.12.cloned.1.call-update) | async-done | bytes 1048592 | tf_op jit(solution)/shard_map/all_gather | solution.py:168
  75.1 1.4 reduce_sum.30
  76.5 1.0 pad_maximum_fusion.4
  77.5 1.6 fusion.17
  79.1 1.2 fusion.18
  80.3 2.0 divide_convert_fusion
  82.3 81.1 %all-gather.6.cloned.1.call-done = bf16[4096,512]{0,1:T(8,128)(2,1)} async-done(((bf16[256,512]{0,1:T(8,128)(2,1)}), bf16[4096,512]{0,1:T(8,128)(2,1)}) %all-gather.6.cloned.1.call-update) | async-done | bytes 4194320 | tf_op jit(solution)/shard_map/all_gather | solution.py:194
  163.5 9.7 %while.15 = (s32[]{:T(128)}, f32[2,4,256]{2,1,0:T(4,128)S(1)}, f32[2,4,256]{2,1,0:T(4,128)S(1)}, f32[2,4,256,128]{3,2,1,0:T(8,128)S(1)}, s32[]{:T(128)}, /*index...) while((s32[]{:T(128)}, f32[2,4,256]{2,1,0:T(4,128)S(1)}, ...), condition=%wide.region_6.9_spmd.clone, body=%wide.region_3.8_spmd.clone.sunk | while | flops 551162624 | bytes 33167600 | solution.py:213
  163.9 1.8 fusion.58
  165.8 1.9 copy-done
  167.7 1.0 fusion.59
  168.8 4.4 %fusion.60 = f32[2,4,256,128]{3,2,1,0:T(8,128)S(1)} fusion(f32[2,512,256,4]{2,1,3,0:T(8,128)} %copy-done, f32[2,4,256]{2,1,0:T(4,128)S(1)} %max.13, pred[256,512]{0,1:T(8,128)(4,1)S(1)} %broadcast_compare_fusion.3, f32[2,4,256,128]{3,2,1,0:T(8,128)S(1)} %get-tuple-element.231, f32[2,4,256]{2,1,0:T(4,128)S(1)} %bitcast.165, ...), kind=kOutput, calls=%fused_computation.13.clone.1 | convolution fusion | flops 274202624 | bytes 6701064 | tf_op jit(solution)/shard_map/while/body/hgrk,khd->hgrd/dot_general | solution.py:58
  173.2 0.3 divide_convert_fusion.1
  173.9 1.0 sort.35
  175.0 1.4 collective-permute-done.3
  176.7 0.7 gather_fusion
  177.7 1.3 copy.42
  179.0 64.7 %all-gather.10.cloned.1.call-done = bf16[2048,1024]{1,0:T(8,128)(2,1)} async-done(((bf16[2048,256]{1,0:T(8,128)(2,1)}), bf16[2048,1024]{1,0:T(8,128)(2,1)}) %all-gather.10.cloned.1.call-update) | async-done | bytes 4194320 | tf_op jit(solution)/shard_map/all_gather | solution.py:245
  243.8 52.3 %all-gather.8.cloned.1.call-done = bf16[1024,2048]{0,1:T(8,128)(2,1)} async-done(((bf16[256,2048]{0,1:T(8,128)(2,1)}), bf16[1024,2048]{0,1:T(8,128)(2,1)}) %all-gather.8.cloned.1.call-update) | async-done | bytes 4194320 | tf_op jit(solution)/shard_map/all_gather | solution.py:244
  296.1 10.0 %fusion.47 = f32[1024,1024]{1,0:T(8,128)} fusion(bf16[1024,2048]{0,1:T(8,128)(2,1)} %all-gather.8.cloned.1.call-done, bf16[2048,1024]{1,0:T(8,128)(2,1)} %all-gather.10.cloned.1.call-done), kind=kOutput, calls=%fused_computation.105 | convolution fusion | flops 4294967296 | bytes 12582912 | tf_op jit(solution)/shard_map/dot_general | solution.py:246
  306.1 12.0 %reduce-scatter.2.cloned.1.call-done = f32[1024,512]{1,0:T(8,128)} async-done(((f32[1024,1024]{1,0:T(8,128)}), f32[1024,512]{1,0:T(8,128)}) %reduce-scatter.2.cloned.1.call-update) | async-done | bytes 2097168 | tf_op jit(solution)/shard_map/reduce_scatter | solution.py:247
  318.2 1.7 convert_element_type.45
  319.9 18.3 %all_to_all.5 = bf16[4,256,512]{2,1,0:T(8,128)(2,1)S(1)} all-to-all(bf16[4,256,512]{2,1,0:T(8,128)(2,1)S(1)} %bitcast.149), channel_id=1, replica_groups=mesh['cz'=4,'cb'=4,'head'=2] {'cb'}, dimensions={0} | all-to-all | bytes 2097152 | tf_op jit(solution)/shard_map/all_to_all | solution.py:250
  338.2 0.3 reshape.220
  338.5 1.4 copy.63
  339.8 1.6 reshape.221
  (72 shorter events, 3.1 us)
Async XLA Ops:
  6.5 68.5 %all-gather.12.cloned.1.call-start = ((), (), s32[]{:S(2)}) async-start(), calls=%async_computation.6 | async-start | bytes 1114112 | tf_op jit(solution)/shard_map/all_gather | solution.py:168
  10.6 2.4 collective-permute-start
  12.9 0.6 copy-start.2
  13.0 3.4 copy-start.6
  13.0 3.4 copy-start.7
  13.0 3.4 copy-start.4
  13.2 4.3 %copy-start.1 = (bf16[256,2048]{1,0:T(8,128)(2,1)S(1)}, bf16[256,2048]{1,0:T(8,128)(2,1)}, u32[]{:S(2)}) copy-start(bf16[256,2048]{1,0:T(8,128)(2,1)} %param.13) | copy-start | bytes 3145732
  15.6 147.9 %all-gather.6.cloned.1.call-start = ((), (), s32[]{:S(2)}) async-start(), calls=%async_computation.2 | async-start | bytes 4456448 | tf_op jit(solution)/shard_map/all_gather | solution.py:194
  15.7 0.6 copy-start.5
  17.3 226.5 %all-gather.10.cloned.1.call-start = ((), (), s32[]{:S(2)}) async-start(), calls=%async_computation.4 | async-start | bytes 5242880 | tf_op jit(solution)/shard_map/all_gather | solution.py:245
  20.8 6.0 %collective-permute-start.1 = (bf16[256,4,4,128]{3,0,2,1:T(8,128)(2,1)S(1)}, bf16[256,4,4,128]{3,0,2,1:T(8,128)(2,1)S(1)}, u32[]{:S(2)}, u32[]{:S(2)}) collective-permute-start(bf16[256,4,4,128]{3,0,2,1:T(8,128)(2,1)S(1)} %bitcast.147), channel_id=1, source_target_pairs={{0,1},{1,0},{2,3},{3,2},{4,5},{5,4},{6,7},{7,6},{8,9},{9,8},{10,11... | collective-permute-start | bytes 3145736 | tf_op jit(solution)/shard_map/ppermute | solution.py:135
  20.9 275.2 %all-gather.8.cloned.1.call-start = ((), (), s32[]{:S(2)}) async-start(), calls=%async_computation.3 | async-start | bytes 5242880 | tf_op jit(solution)/shard_map/all_gather | solution.py:244
  21.3 55.2 %collective-permute-start.2 = (bf16[256,2,2,128]{3,0,1,2:T(8,128)(2,1)S(1)}, bf16[256,2,2,128]{3,0,1,2:T(8,128)(2,1)}, u32[]{:S(2)}, u32[]{:S(2)}) collective-permute-start(bf16[256,2,2,128]{3,0,1,2:T(8,128)(2,1)S(1)} %fusion.32), channel_id=1, source_target_pairs={{0,2},{2,4},{4,6},{6,8},{8,10},{10,12},{12,14},{14,16},{16,18},{18... | collective-permute-start | bytes 786440 | tf_op jit(solution)/shard_map/ppermute | solution.py:166
  163.5 10.2 %copy-start.3 = (s32[8]{0:T(128)S(1)}, s32[8]{0:T(128)}, u32[]{:S(2)}) copy-start(s32[8]{0:T(128)} %copy-done.2) | copy-start | bytes 100
  165.8 2.0 copy-start
  173.7 2.7 collective-permute-start.3
  179.0 139.2 %reduce-scatter.2.cloned.1.call-start = ((), (), s32[]{:S(2)}) async-start(), calls=%async_computation.5 | async-start | bytes 6291456 | tf_op jit(solution)/shard_map/reduce_scatter | solution.py:247
Sparse Core Ops, SparseCore 0:
  15.7 59.2 all-gather.11
  77.8 85.6 all-gather.5
  165.0 78.7 all-gather.9
  245.5 50.6 all-gather.7
  306.3 11.8 reduce-scatter.1
